TPU v7x, 256 devices: a whole 4x4x8 slice. The times are simulated.
256 devices in a mesh: ctx: 32 (over z_hi, x, y), head: 8 (over z_lo, core).
Axes of the slice: x: 4, y: 4, z: 8 (z_hi: 2, z_lo: 4; z = z_hi * 4 + z_lo), core: 2. Of those that a mesh axis runs over, the one named last changes fastest.
Arguments:
- queries: bfloat16 [12288, 4096], P('ctx', 'head'), may hold values from -200 to 200
- key_matrix: bfloat16 [12288, 1024], P('ctx', 'head'), may hold values from -6 to 6
- value_matrix: bfloat16 [12288, 1024], P('ctx', 'head'), may hold values from -6 to 6
- doc_ids: int32 [12288], P('ctx'), may hold values from 0 to 15, never falling along the last dimension, each value on 1 to 6528 neighbouring positions
- out_weight: bfloat16 [4096, 4096], P('head'), may hold values from -0.09375 to 0.09375
Outputs:
- projected: bfloat16 [12288, 4096], P(('ctx', 'head'))
Inputs may be any that keep to these rules, and one draw needn't show every extreme that they name: `doc_ids`: document ids never fall along the tokens; each document has 1 to 6528 tokens and one has exactly 6528.
All inputs are finite; a program needn't handle non-finite values.
Results may differ from a plain program's by a relative error of at most 0.019.
Values may be sent and summed in bfloat16 or wider, within the bound.
No kernel may reach another device: no remote copies, remote signals or barrier semaphores. Data moves between devices by JAX's collectives and lax.ppermute only.
A program may use at most 256 MiB of HBM per device.

v0:
```python
import jax
import jax.numpy as jnp
from jax import lax
from jax.sharding import PartitionSpec as P

HEAD_WIDTH = 128


def per_device(queries, key_matrix, value_matrix, doc_ids, out_weight):
    tok_rows = queries.shape[0]
    kv_here = key_matrix.shape[1] // HEAD_WIDTH
    queries_per_group = queries.shape[1] // key_matrix.shape[1]
    all_rows = queries_per_group * tok_rows
    my_index = lax.axis_index("ctx")
    q_pos = my_index * tok_rows + jnp.arange(tok_rows, dtype=jnp.int32)
    q_rows = (
        queries.reshape(tok_rows, kv_here, queries_per_group, HEAD_WIDTH)
        .transpose(1, 2, 0, 3)
        .reshape(kv_here, all_rows, HEAD_WIDTH)
    )
    score_scale = HEAD_WIDTH ** (-0.5)
    running = jnp.full((kv_here, all_rows), -1e30, jnp.float32)
    part_keys = lax.all_gather(key_matrix, "ctx", axis=0, tiled=True)
    part_values = lax.all_gather(value_matrix, "ctx", axis=0, tiled=True)
    part_docs = lax.all_gather(doc_ids, "ctx", axis=0, tiled=True)
    key_count = part_keys.shape[0]
    k_pos = jnp.arange(key_count, dtype=jnp.int32)
    keys_three = part_keys.reshape(key_count, kv_here, HEAD_WIDTH).transpose(1, 0, 2)
    values_three = part_values.reshape(key_count, kv_here, HEAD_WIDTH).transpose(1, 0, 2)
    scores = (
        jnp.einsum("hqd,hkd->hqk", q_rows, keys_three, preferred_element_type=jnp.float32)
        * score_scale
    )
    allowed = (
        (doc_ids[:, None] == part_docs[None, :])
        & (q_pos[:, None] >= k_pos[None, :])
        & (k_pos[None, :] >= 0)
    )
    allowed = jnp.tile(allowed, (queries_per_group, 1))[None]
    scores = jnp.where(allowed, scores, jnp.float32(-1e30))
    new_max = jnp.maximum(running, jnp.max(scores, axis=-1))
    weights = jnp.where(allowed, jnp.exp(scores - new_max[..., None]), jnp.float32(0.0))
    denominator = jnp.sum(weights, axis=-1)
    weighted = jnp.einsum(
        "hqk,hkd->hqd",
        weights.astype(jnp.bfloat16),
        values_three,
        preferred_element_type=jnp.float32,
    )
    running_state = (new_max, denominator, weighted)
    running, denominator, weighted = running_state
    attended = (weighted / denominator[..., None]).astype(jnp.bfloat16)
    attended = (
        attended.reshape(kv_here, queries_per_group, tok_rows, HEAD_WIDTH)
        .transpose(2, 0, 1, 3)
        .reshape(tok_rows, kv_here * queries_per_group * HEAD_WIDTH)
    )
    return lax.psum_scatter(
        jnp.dot(attended, out_weight, preferred_element_type=jnp.float32).astype(jnp.bfloat16),
        "head",
        scatter_dimension=0,
        tiled=True,
    )


def solution(mesh):
    placed = (P("ctx", "head"), P("ctx", "head"), P("ctx", "head"), P("ctx"), P("head", None))
    return jax.shard_map(
        per_device, mesh=mesh, in_specs=placed, out_specs=P(("ctx", "head"), None), check_vma=False
    )
```

profile of v0, /device:TPU:2, one launch (start us, length us, event | category | flops | bytes accessed | tf_op | source)
XLA Modules:
  0.0 284.2 jit_solution(17755640284244588646)
XLA Ops:
  6.5 0.0 all-gather.4.cloned.1.call-start
  6.5 0.7 all-gather.4.cloned.1.call-update
  7.3 0.0 all-gather.6.cloned.1.call-start
  7.3 0.7 all-gather.6.cloned.1.call-update
  8.0 0.0 reduce-scatter.2.cloned.1.call-start
  8.1 0.7 reshape.107
  8.7 1.2 copy.10
  10.0 0.2 copy.11
  10.2 109.3 %all-gather = s32[32,1,384]{2,1,0:T(1,128)S(1)} all-gather(s32[1,1,384]{2,1,0:T(1,128)S(1)} %reshape.107), channel_id=1, replica_groups=mesh['ctx'=32,'head'=8] {'ctx'}, dimensions={0}, use_global_device_ids=true | all-gather | bytes 50688 | tf_op jit(solution)/shard_map/all_gather | solution.py:25
  119.5 9.4 %fusion.3 = pred[384,12288]{1,0:T(8,128)(4,1)} fusion(s32[384]{0:T(512)S(1)} %iota_add_fusion, s32[12288]{0:T(1024)S(1)} %bitcast.30, s32[384]{0:T(512)} %param.8), kind=kLoop, calls=%fused_computation.6 | loop fusion | flops 14155776 | bytes 4770816 | tf_op jit(solution)/shard_map/and | solution.py:35
  128.9 0.0 all-gather.4.cloned.1.call-done
  128.9 30.1 %fusion = (f32[1536]{0:T(1024)S(1)}, f32[1536,12288]{1,0:T(8,128)}) fusion(pred[384,12288]{1,0:T(8,128)(4,1)} %fusion.3, bf16[1536,128]{1,0:T(8,128)(2,1)S(1)} %bitcast.26, bf16[12288,128]{1,0:T(8,128)(2,1)} %all-gather.4.cloned.1.call-done), kind=kOutput, calls=%fused_computation.2 | convolution fusion | flops 4888459776 | bytes 83761152 | tf_op jit(solution)/shard_map/hqd,hkd->hqk/dot_general | solution.py:31
  159.0 40.9 %fusion.1 = (f32[1536]{0:T(1024)S(1)}, bf16[1536,12288]{1,0:T(8,128)(2,1)}) fusion(f32[1536,12288]{1,0:T(8,128)} %get-tuple-element.8, f32[1536]{0:T(1024)S(1)} %broadcast_maximum_fusion, pred[384,12288]{1,0:T(8,128)(4,1)} %fusion.3), kind=kLoop, calls=%fused_computation.3 | loop fusion | flops 113244672 | bytes 117977088 | tf_op jit(solution)/shard_map/reduce_sum | solution.py:43
  199.9 12.3 %all-gather.6.cloned.1.call-done = bf16[12288,128]{1,0:T(8,128)(2,1)} async-done(((bf16[384,128]{1,0:T(8,128)(2,1)}), bf16[12288,128]{1,0:T(8,128)(2,1)}) %all-gather.6.cloned.1.call-update) | async-done | bytes 3145744 | tf_op jit(solution)/shard_map/all_gather | solution.py:24
  212.2 17.7 %fusion.4 = bf16[1536,128]{1,0:T(8,128)(2,1)S(1)} fusion(bf16[1536,12288]{1,0:T(8,128)(2,1)} %get-tuple-element.6, bf16[12288,128]{1,0:T(8,128)(2,1)} %all-gather.6.cloned.1.call-done, f32[1536]{0:T(1024)S(1)} %get-tuple-element.5), kind=kOutput, calls=%fused_computation.9 | convolution fusion | flops 4832231424 | bytes 41293824 | tf_op jit(solution)/shard_map/hqk,hkd->hqd/dot_general | solution.py:44
  229.9 0.2 copy.12
  230.1 5.7 %convolution_convert_fusion = bf16[384,4096]{1,0:T(8,128)(2,1)} fusion(bf16[384,512]{0,1:T(8,128)(2,1)S(1)} %bitcast.28, bf16[512,4096]{1,0:T(8,128)(2,1)} %param.9), kind=kOutput, calls=%fused_computation.7 | convolution fusion | flops 1612185600 | bytes 7733248 | tf_op jit(solution)/shard_map/dot_general | solution.py:59
  235.8 0.0 reduce-scatter.2.cloned.1.call-update
  235.8 41.8 %reduce-scatter.2.cloned.1.call-done = bf16[48,4096]{1,0:T(8,128)(2,1)} async-done(((bf16[384,4096]{1,0:T(8,128)(2,1)}), bf16[48,4096]{1,0:T(8,128)(2,1)}) %reduce-scatter.2.cloned.1.call-update) | async-done | bytes 393232 | tf_op jit(solution)/shard_map/reduce_scatter | solution.py:58
  (2 shorter events, 0.0 us)
Async XLA Ops:
  6.5 122.3 %all-gather.4.cloned.1.call-start = ((), (), s32[]{:S(2)}) async-start(), calls=%async_computation.1 | async-start | bytes 3244032 | tf_op jit(solution)/shard_map/all_gather | solution.py:23
  7.3 204.9 %all-gather.6.cloned.1.call-start = ((), (), s32[]{:S(2)}) async-start(), calls=%async_computation.2 | async-start | bytes 3244032 | tf_op jit(solution)/shard_map/all_gather | solution.py:24
  8.0 269.6 %reduce-scatter.2.cloned.1.call-start = ((), (), s32[]{:S(2)}) async-start(), calls=%async_computation.3 | async-start | bytes 3538944 | tf_op jit(solution)/shard_map/reduce_scatter | solution.py:58
Sparse Core Ops, SparseCore 0:
  10.8 103.0 all-gather.3
  117.2 94.9 all-gather.5
  236.0 41.6 reduce-scatter.1
where the time goes:
time: 284 us
  blocking collectives  109 us (38%)
  waiting for transfers between devices  55.5 us (20%)
  matrix products  53.5 us (19%)
  other arithmetic  50.3 us (18%)
  between operations  13.1 us (5%)
    all_gather x1, blocking collectives, per_device(): part_docs = lax.all_gather(doc_ids, 'ctx', axis=0, tiled=True)  109 us
    reduce_scatter x1, waiting for transfers between devices, per_device(): lax.psum_scatter(jnp.dot(attended, out_weight, preferred_element_type=jnp...  41.8 us
    reduce_sum x1, other arithmetic, per_device(): denominator = jnp.sum(weights, axis=-1)  40.9 us
    dot_general x1, matrix products, per_device(): jnp.einsum('hqd,hkd->hqk', q_rows, keys_three, preferred_element_type=jnp...  30.1 us
    dot_general x1, matrix products, per_device(): jnp.einsum('hqk,hkd->hqd', weights.astype(jnp.bfloat16), values_three, pr...  17.7 us
    all_gather x1, waiting for transfers between devices, per_device(): part_values = lax.all_gather(value_matrix, 'ctx', axis=0, tiled=True)  12.3 us
    and x1, other arithmetic, per_device(): (doc_ids[:, None] == part_docs[None, :]) & (q_pos[:, None] >= k_pos[None,...  9.37 us
  transfers between devices with their start and end apart: 3, of which 2 were waited for; matrix products, arithmetic and copies ran while one was open for 29% of the time, Pallas kernels for 0%

commit v1 on v0

--- a/solution.py
+++ b/solution.py
@@ -20,8 +20,13 @@
     )
     score_scale = HEAD_WIDTH ** (-0.5)
     running = jnp.full((kv_here, all_rows), -1e30, jnp.float32)
-    part_keys = lax.all_gather(key_matrix, "ctx", axis=0, tiled=True)
-    part_values = lax.all_gather(value_matrix, "ctx", axis=0, tiled=True)
+    part_keys, part_values = jnp.split(
+        lax.all_gather(
+            jnp.concatenate([key_matrix, value_matrix], axis=1), "ctx", axis=0, tiled=True
+        ),
+        [key_matrix.shape[1]],
+        axis=1,
+    )
     part_docs = lax.all_gather(doc_ids, "ctx", axis=0, tiled=True)
     key_count = part_keys.shape[0]
     k_pos = jnp.arange(key_count, dtype=jnp.int32)

time: 284 us -> 330 us (1.16)
  local copies, waits for them, and re-layouts: 2.34 us -> 37.9 us
  matrix products: 53.5 us -> 75.4 us
  other arithmetic: 50.3 us -> 38.3 us
  waiting for transfers between devices: 55.5 us -> 60.7 us
  blocking collectives: 109 us -> 104 us
    reduce_scatter x1, waiting for transfers between devices: 41.8 us -> 60.7 us  [per_device(): lax.psum_scatter(jnp.dot(attended, out_weight, preferred_element_type=jnp...]
    another operation x0 -> x1, local copies, waits for them, and re-layouts: none -> 18.9 us  [per_device(): allowed = jnp.tile(allowed, (queries_per_group, 1))[None]]
    dot_general x1, matrix products: 17.7 us -> 35.4 us  [per_device(): jnp.einsum('hqk,hkd->hqd', weights.astype(jnp.bfloat16), values_three, pr...]
    unnamed x2 -> x3, local copies, waits for them, and re-layouts: 1.89 us -> 18.6 us
    all_gather x2 -> x1, waiting for transfers between devices: 12.3 us -> 0.01 us  [per_device(): lax.all_gather(jnp.concatenate([key_matrix, value_matrix], axis=1), 'ctx'...]
    reduce_sum x1, other arithmetic: 40.9 us -> 30 us  [per_device(): denominator = jnp.sum(weights, axis=-1)]
    all_gather x1, blocking collectives: 109 us -> 104 us  [per_device(): part_docs = lax.all_gather(doc_ids, 'ctx', axis=0, tiled=True)]
    dot_general x1, matrix products: 30.1 us -> 34.3 us  [per_device(): jnp.einsum('hqd,hkd->hqk', q_rows, keys_three, preferred_element_type=jnp...]
  transfers between devices with their start and end apart: 3 -> 2, of which waited for: 2 -> 1; matrix products, arithmetic and copies ran while one was open for 29% -> 13% of each run, Pallas kernels for 0% -> 0%
where the time goes in v1:
time: 330 us
  blocking collectives  104 us (32%)
  matrix products  75.4 us (23%)
  waiting for transfers between devices  60.7 us (18%)
  other arithmetic  38.3 us (12%)
  local copies, waits for them, and re-layouts  37.9 us (11%)
  between operations  13.4 us (4%)
    all_gather x1, blocking collectives, per_device(): part_docs = lax.all_gather(doc_ids, 'ctx', axis=0, tiled=True)  104 us
    reduce_scatter x1, waiting for transfers between devices, per_device(): lax.psum_scatter(jnp.dot(attended, out_weight, preferred_element_type=jnp...  60.7 us
    dot_general x1, matrix products, per_device(): jnp.einsum('hqk,hkd->hqd', weights.astype(jnp.bfloat16), values_three, pr...  35.4 us
    dot_general x1, matrix products, per_device(): jnp.einsum('hqd,hkd->hqk', q_rows, keys_three, preferred_element_type=jnp...  34.3 us
    reduce_sum x1, other arithmetic, per_device(): denominator = jnp.sum(weights, axis=-1)  30 us
    another operation x1, local copies, waits for them, and re-layouts, per_device(): allowed = jnp.tile(allowed, (queries_per_group, 1))[None]  18.9 us
    unnamed x3, local copies, waits for them, and re-layouts  18.6 us
    and x1, other arithmetic, per_device(): (doc_ids[:, None] == part_docs[None, :]) & (q_pos[:, None] >= k_pos[None,...  6.68 us
  transfers between devices with their start and end apart: 2, of which 1 were waited for; matrix products, arithmetic and copies ran while one was open for 13% of the time, Pallas kernels for 0%

profile of v1, /device:TPU:2, one launch (start us, length us, event | category | flops | bytes accessed | tf_op | source)
XLA Modules:
  0.0 330.0 jit_solution(15331709175194100001)
XLA Ops:
  6.5 0.0 all-gather.3.cloned.1.call-start
  6.5 1.6 pad_maximum_fusion
  8.2 0.0 all-gather.3.cloned.1.call-update
  8.2 0.0 reduce-scatter.2.cloned.1.call-start
  8.3 0.7 reshape.107
  8.9 1.2 copy.10
  10.2 0.2 copy.11
  10.4 104.2 %all-gather = s32[32,1,384]{2,1,0:T(1,128)S(1)} all-gather(s32[1,1,384]{2,1,0:T(1,128)S(1)} %reshape.107), channel_id=1, replica_groups=mesh['ctx'=32,'head'=8] {'ctx'}, dimensions={0}, use_global_device_ids=true | all-gather | bytes 50688 | tf_op jit(solution)/shard_map/all_gather | solution.py:30
  114.6 6.7 %fusion.5 = pred[384,12288]{0,1:T(8,128)(4,1)S(1)} fusion(s32[384]{0:T(512)S(1)} %iota_add_fusion, s32[384]{0:T(512)} %param.8, s32[12288]{0:T(1024)S(1)} %bitcast.39), kind=kLoop, calls=%fused_computation.7 | loop fusion | flops 14155776 | bytes 4770816 | tf_op jit(solution)/shard_map/and | solution.py:40
  121.3 18.9 %tile.8 = pred[4,384,12288]{1,0,2:T(4,128)(4,1)} broadcast(pred[384,12288]{0,1:T(8,128)(4,1)S(1)} %fusion.5), dimensions={1,2} | broadcast | bytes 23592960 | tf_op jit(solution)/shard_map/tile | solution.py:44
  140.1 16.7 %copy.13 = pred[1536,8,4,384]{3,1,2,0:T(8,128)(4,1)} copy(pred[1536,8,4,384]{3,2,1,0:T(4,128)(4,1)} %bitcast.31) | data formatting | bytes 37748736
  156.8 0.0 all-gather.3.cloned.1.call-done
  156.9 34.3 %fusion = (f32[1536]{0:T(1024)S(1)}, f32[12288,1536]{1,0:T(8,128)}) fusion(pred[1536,12288]{0,1:T(8,128)(4,1)} %bitcast.32, bf16[1536,128]{1,0:T(8,128)(2,1)S(1)} %bitcast.37, bf16[12288,256]{1,0:T(8,128)(2,1)} %all-gather.3.cloned.1.call-done), kind=kOutput, calls=%fused_computation.2 | convolution fusion | flops 4888459776 | bytes 97916928 | tf_op jit(solution)/shard_map/hqd,hkd->hqk/dot_general | solution.py:36
  191.2 30.0 %fusion.1 = f32[1536]{0:T(1024)S(1)} fusion(pred[1536,12288]{0,1:T(8,128)(4,1)} %bitcast.33, f32[12288,1536]{1,0:T(8,128)} %get-tuple-element.6, f32[1536]{0:T(1024)S(1)} %broadcast_maximum_fusion), kind=kLoop, calls=%fused_computation.3 | loop fusion | flops 94370304 | bytes 94384128 | tf_op jit(solution)/shard_map/reduce_sum | solution.py:48
  221.1 35.4 %fusion.14 = bf16[1536,128]{1,0:T(8,128)(2,1)S(1)} fusion(bf16[12288,256]{1,0:T(8,128)(2,1)} %all-gather.3.cloned.1.call-done, pred[1536,12288]{0,1:T(8,128)(4,1)} %bitcast.34, f32[12288,1536]{1,0:T(8,128)} %get-tuple-element.6, f32[1536]{0:T(1024)S(1)} %broadcast_maximum_fusion, f32[1536]{0:T(1024)S(1)} %fusion.1), kind=kOutput, calls=%fused_computation.13 | convolution fusion | flops 4926603264 | bytes 97923072 | tf_op jit(solution)/shard_map/hqk,hkd->hqd/dot_general | solution.py:49
  256.6 0.2 copy.12
  256.8 5.7 %convolution_convert_fusion = bf16[384,4096]{1,0:T(8,128)(2,1)} fusion(bf16[384,512]{0,1:T(8,128)(2,1)S(1)} %bitcast.36, bf16[512,4096]{1,0:T(8,128)(2,1)} %param.9), kind=kOutput, calls=%fused_computation.8 | convolution fusion | flops 1612185600 | bytes 7733248 | tf_op jit(solution)/shard_map/dot_general | solution.py:64
  262.5 0.0 reduce-scatter.2.cloned.1.call-update
  262.5 60.7 %reduce-scatter.2.cloned.1.call-done = bf16[48,4096]{1,0:T(8,128)(2,1)} async-done(((bf16[384,4096]{1,0:T(8,128)(2,1)}), bf16[48,4096]{1,0:T(8,128)(2,1)}) %reduce-scatter.2.cloned.1.call-update) | async-done | bytes 393232 | tf_op jit(solution)/shard_map/reduce_scatter | solution.py:63
  (2 shorter events, 0.0 us)
Async XLA Ops:
  6.5 150.3 %all-gather.3.cloned.1.call-start = ((), (), s32[]{:S(2)}) async-start(), calls=%async_computation.1 | async-start | bytes 6488064 | tf_op jit(solution)/shard_map/all_gather | solution.py:24
  8.2 315.0 %reduce-scatter.2.cloned.1.call-start = ((), (), s32[]{:S(2)}) async-start(), calls=%async_computation.2 | async-start | bytes 3538944 | tf_op jit(solution)/shard_map/reduce_scatter | solution.py:63
Sparse Core Ops, SparseCore 0:
  10.8 134.7 all-gather.2
  262.6 60.5 reduce-scatter.1
